TPU v7x, 256 devices: a whole 4x4x8 slice. The times are simulated.
256 devices in a mesh: cfg: 2 (over z_lo), req: 16 (over y, z_hi), mlp: 8 (over x, core).
Axes of the slice: x: 4, y: 4, z: 8 (z_hi: 4, z_lo: 2; z = z_hi * 2 + z_lo), core: 2. Of those that a mesh axis runs over, the one named last changes fastest.
Arguments:
- hidden: bfloat16 [2, 16384, 1152], P('cfg', ('req', 'mlp')), may hold values from -64 to 64
- noisy_latent: float32 [16384, 16], P(('req', 'mlp'), 'cfg'), may hold values from -6 to 6
- labels: int32 [16, 4], replicated, may hold values from 0 to 999
- timesteps: int32 [16, 4], replicated, may hold values from 0 to 999
- lengths: int32 [16, 4], P('req'), may hold values from 1 to 512, 1024 in all within a row
- guidance: float32 [16, 4], P('req'), may hold values from 1.5 to 4
- keep_scale: float32 [16, 4], P('req'), may hold values from 0.9 to 1.2
- noise_scale: float32 [16, 4], P('req'), may hold values from -0.8 to -0.2
- class_table: bfloat16 [1001, 1152], replicated, may hold values from -6 to 6
- time_up: bfloat16 [256, 1152], replicated, may hold values from -0.375 to 0.375
- time_up_bias: bfloat16 [1152], replicated, may hold values from -4 to 4
- time_out: bfloat16 [1152, 1152], replicated, may hold values from -0.1875 to 0.1875
- time_out_bias: bfloat16 [1152], replicated, may hold values from -4 to 4
- mod_weight: bfloat16 [1152, 9216], P(None, 'req'), may hold values from -0.1875 to 0.1875
- mod_bias: bfloat16 [9216], P('req'), may hold values from -4 to 4
- qkv_weight: bfloat16 [1152, 3456], P(None, 'req'), may hold values from -8 to 8
- qkv_bias: bfloat16 [3456], P('req'), may hold values from -4 to 4
- out_weight: bfloat16 [1152, 1152], P(None, 'req'), may hold values from -0.1875 to 0.1875
- out_bias: bfloat16 [1152], P('req'), may hold values from -4 to 4
- up_weight: bfloat16 [1152, 4608], P(None, 'mlp'), may hold values from -0.1875 to 0.1875
- up_bias: bfloat16 [4608], P('mlp'), may hold values from -4 to 4
- down_weight: bfloat16 [4608, 1152], P('mlp'), may hold values from -1 to 1
- down_bias: bfloat16 [1152], replicated, may hold values from -4 to 4
- final_weight: bfloat16 [1152, 16], replicated, may hold values from -0.1875 to 0.1875
- final_bias: bfloat16 [16], replicated, may hold values from -4 to 4
Outputs:
- next_latent: float32 [16384, 16], P(('req', 'mlp'), 'cfg')
Inputs may be any that keep to these rules, and one draw needn't show every extreme that they name: `lengths`: each row sums to 1024, and its largest crop has exactly 512 tokens.
All inputs are finite; a program needn't handle non-finite values.
Results may differ from a plain program's by a relative error of at most 0.015.
Values may be sent and summed in bfloat16 or wider, within the bound.
No kernel may reach another device: no remote copies, remote signals or barrier semaphores. Data moves between devices by JAX's collectives and lax.ppermute only.
A program may use at most 128 MiB of HBM per device.

v0:
```python
import math
import jax
import jax.numpy as jnp
from jax import lax
from jax.sharding import PartitionSpec as P

HEADS = 16
HEAD_DIM = 72
CLASSES = 1000
FREQ = 256


def layer_norm(values):
    values = values.astype(jnp.float32)
    centre = values - jnp.mean(values, axis=-1, keepdims=True)
    variance = jnp.mean(centre * centre, axis=-1, keepdims=True)
    return centre * lax.rsqrt(variance + 1e-06)


def time_features(times_flat):
    half_freq = FREQ // 2
    frequency = jnp.exp(-math.log(10000.0) * jnp.arange(half_freq, dtype=jnp.float32) / half_freq)
    angles = times_flat.astype(jnp.float32)[:, None] * frequency[None, :]
    return jnp.concatenate([jnp.cos(angles), jnp.sin(angles)], axis=1).astype(jnp.bfloat16)


def segment_ids(lengths_row, positions):
    ends = jnp.cumsum(lengths_row)
    return jnp.sum((positions[:, None] >= ends[None, :]).astype(jnp.int32), axis=1)


def attention(queries, keys_all, values_all, query_segment, key_segment):
    scores = jnp.einsum(
        "qhd,khd->hqk", queries, keys_all, preferred_element_type=jnp.float32
    ) / math.sqrt(HEAD_DIM)
    same = (query_segment[:, None] == key_segment[None, :])[None]
    masked = jnp.where(same, scores, -1e30)
    row_max = jnp.max(masked, axis=2, keepdims=True)
    expo = jnp.where(same, jnp.exp(masked - row_max), 0.0)
    denominator = jnp.sum(expo, axis=2)
    weights = expo.astype(jnp.bfloat16)
    mixed = jnp.einsum("hqk,khd->qhd", weights, values_all, preferred_element_type=jnp.float32)
    result = mixed / jnp.transpose(denominator)[:, :, None]
    return result.astype(jnp.bfloat16).reshape(queries.shape[0], -1)


def shards(
    hidden,
    noisy_latent,
    labels,
    timesteps,
    lengths,
    guidance,
    keep_scale,
    noise_scale,
    class_table,
    time_up,
    time_up_bias,
    time_out,
    time_out_bias,
    mod_weight,
    mod_bias,
    qkv_weight,
    qkv_bias,
    out_weight,
    out_bias,
    up_weight,
    up_bias,
    down_weight,
    down_bias,
    final_weight,
    final_bias,
):
    req_count = lax.axis_size("req")
    mlp_count = lax.axis_size("mlp")
    half_index = lax.axis_index("cfg")
    mlp_index = lax.axis_index("mlp")
    tok_rows = hidden.shape[1]
    width = hidden.shape[2]
    group_rows = tok_rows * mlp_count
    per_group = labels.shape[1]
    time_feat = time_features(timesteps.reshape(-1))
    time_mid = jax.nn.silu(
        jnp.dot(time_feat, time_up, preferred_element_type=jnp.float32)
        + time_up_bias.astype(jnp.float32)
    ).astype(jnp.bfloat16)
    time_cond = jnp.dot(
        time_mid, time_out, preferred_element_type=jnp.float32
    ) + time_out_bias.astype(jnp.float32)
    used_labels = jnp.where(half_index == 0, labels.reshape(-1), CLASSES)
    one_hot = (used_labels[:, None] == jnp.arange(CLASSES + 1, dtype=jnp.int32)[None, :]).astype(
        jnp.bfloat16
    )
    cond_act = jax.nn.silu(
        time_cond + jnp.dot(one_hot, class_table, preferred_element_type=jnp.float32)
    ).astype(jnp.bfloat16)
    local_mod = (
        jnp.dot(cond_act, mod_weight, preferred_element_type=jnp.float32)
        + mod_bias.astype(jnp.float32)
    ).astype(jnp.bfloat16)
    local_mod = local_mod.reshape(req_count, per_group, local_mod.shape[1])
    modulation = lax.all_to_all(local_mod, "req", split_axis=0, concat_axis=2, tiled=True)[0]
    positions = jnp.arange(group_rows, dtype=jnp.int32)
    segment_all = segment_ids(lengths[0], positions)
    segment_own = lax.dynamic_slice_in_dim(segment_all, mlp_index * tok_rows, tok_rows)
    member = segment_own[:, None] == jnp.arange(per_group, dtype=jnp.int32)[None, :]
    per_token = jnp.dot(member.astype(jnp.bfloat16), modulation, preferred_element_type=jnp.float32)
    pieces = [per_token[:, index * width : (index + 1) * width] for index in range(8)]
    shift_attn, scale_attn, gate_attn, shift_mlp, scale_mlp, gate_mlp, shift_final, scale_final = (
        pieces
    )
    rows = hidden[0]
    normed = (layer_norm(rows) * (1.0 + scale_attn) + shift_attn).astype(jnp.bfloat16)
    qkv_full, qkv_bias_full, out_full, out_bias_full = (
        lax.all_gather(qkv_weight, "req", axis=1, tiled=True),
        lax.all_gather(qkv_bias, "req", axis=0, tiled=True),
        lax.all_gather(out_weight, "req", axis=1, tiled=True),
        lax.all_gather(out_bias, "req", axis=0, tiled=True),
    )
    qkv = (
        jnp.dot(normed, qkv_full, preferred_element_type=jnp.float32)
        + qkv_bias_full.astype(jnp.float32)
    ).astype(jnp.bfloat16)
    keys_all, values_all = (
        lax.all_gather(qkv[:, width : 2 * width], "mlp", axis=0, tiled=True),
        lax.all_gather(qkv[:, 2 * width :], "mlp", axis=0, tiled=True),
    )
    attended = attention(
        qkv[:, :width].reshape(tok_rows, HEADS, HEAD_DIM),
        keys_all.reshape(group_rows, HEADS, HEAD_DIM),
        values_all.reshape(group_rows, HEADS, HEAD_DIM),
        segment_own,
        segment_all,
    )
    projected = jnp.dot(
        attended, out_full, preferred_element_type=jnp.float32
    ) + out_bias_full.astype(jnp.float32)
    mid_hidden = (rows.astype(jnp.float32) + gate_attn * projected).astype(jnp.bfloat16)
    normed_mlp = (layer_norm(mid_hidden) * (1.0 + scale_mlp) + shift_mlp).astype(jnp.bfloat16)
    gathered = lax.all_gather(normed_mlp, "mlp", axis=0, tiled=True)
    inner = jax.nn.gelu(
        jnp.dot(gathered, up_weight, preferred_element_type=jnp.float32)
        + up_bias.astype(jnp.float32),
        approximate=True,
    ).astype(jnp.bfloat16)
    mlp_out = lax.psum_scatter(
        jnp.dot(inner, down_weight, preferred_element_type=jnp.float32).astype(jnp.bfloat16),
        "mlp",
        scatter_dimension=0,
        tiled=True,
    ).astype(jnp.float32)
    final_hidden = mid_hidden.astype(jnp.float32) + gate_mlp * (
        mlp_out + down_bias.astype(jnp.float32)
    )
    normed_final = (layer_norm(final_hidden) * (1.0 + scale_final) + shift_final).astype(
        jnp.bfloat16
    )
    predicted = jnp.dot(
        normed_final, final_weight, preferred_element_type=jnp.float32
    ) + final_bias.astype(jnp.float32)
    halves = lax.all_to_all(predicted[None], "cfg", split_axis=2, concat_axis=0, tiled=True)
    eps_cond = halves[0]
    eps_free = halves[1]
    member_f = member.astype(jnp.float32)
    guide_tok = jnp.sum(member_f * guidance, axis=1, keepdims=True)
    keep_tok = jnp.sum(member_f * keep_scale, axis=1, keepdims=True)
    noise_tok = jnp.sum(member_f * noise_scale, axis=1, keepdims=True)
    return keep_tok * noisy_latent + noise_tok * (eps_free + guide_tok * (eps_cond - eps_free))


def solution(mesh):
    return jax.shard_map(
        shards,
        mesh=mesh,
        in_specs=(
            P("cfg", ("req", "mlp"), None),
            P(("req", "mlp"), "cfg"),
            P(),
            P(),
            P("req", None),
            P("req", None),
            P("req", None),
            P("req", None),
            P(),
            P(),
            P(),
            P(),
            P(),
            P(None, "req"),
            P("req"),
            P(None, "req"),
            P("req"),
            P(None, "req"),
            P("req"),
            P(None, "mlp"),
            P("mlp"),
            P("mlp", None),
            P(),
            P(),
            P(),
        ),
        out_specs=P(("req", "mlp"), "cfg"),
        check_vma=False,
    )
```

profile of v0, /device:TPU:8, one launch (start us, length us, event | category | flops | bytes accessed | tf_op | source)
XLA Modules:
  0.0 357.1 jit_solution(16776291229437060213)
XLA Ops:
  11.4 1.8 convolution_add_fusion.3
  13.2 3.0 fusion.29
  16.9 11.6 %all-to-all-start = ((bf16[16,4,576]{2,1,0:T(4,128)(2,1)}), bf16[16,4,576]{2,1,0:T(4,128)(2,1)S(1)}, u32[]{:S(2)}, u32[]{:S(2)}) async-start(bf16[16,4,576]{2,1,0:T(4,128)(2,1)} %reshape.143), calls=%async_computation | async-start | bytes 163840 | tf_op jit(solution)/shard_map/all_to_all | solution.py:102
  31.1 82.8 %all-reduce.2 = (bf16[3456]{0:T(1024)(128)(2,1)S(1)}, bf16[1152]{0:T(1024)(128)(2,1)S(1)}) all-reduce(bf16[3456]{0:T(1024)(128)(2,1)S(1)} %dynamic-update-slice, bf16[1152]{0:T(1024)(128)(2,1)S(1)} %dynamic-update-slice.1), channel_id=1, replica_groups=mesh['cfg'=2,'req'=16,'mlp'=8] {'req'}, use_global_device_ids=true, to_apply=%add | all-reduce | flops 4608 | bytes 18432
  114.6 3.0 fusion.67
  117.6 6.1 %fusion.2 = bf16[128,3456]{1,0:T(8,128)(2,1)S(1)} fusion(bf16[1152,3456]{0,1:T(8,128)(2,1)} %all-gather.6.cloned.1.call-done, f32[3456]{0:T(1024)S(1)} %convert_element_type.103, bf16[1,128,1152]{2,1,0:T(8,128)(2,1)S(1)} %copy-done.1, f32[128,9216]{1,0:T(8,128)} %fusion.67, f32[128]{0:T(128)S(1)} %add_rsqrt_fusion.2, f32[128]{0:T(128)S(1)} %broadcast_multiply_fusion.2), kind=kOutput, calls=%fused_computation.5 | convolution fusion | flops 1021132800 | bytes 10336768 | tf_op jit(solution)/shard_map/dot_general | solution.py:121
  123.7 0.9 fusion.83
  126.2 0.8 broadcast_compare_fusion
  127.2 37.7 %all-gather.10.cloned.1.call-done = bf16[1024,1152]{1,0:T(8,128)(2,1)} async-done(((bf16[128,1152]{1,0:T(8,128)(2,1)}), bf16[1024,1152]{1,0:T(8,128)(2,1)}) %all-gather.10.cloned.1.call-update) | async-done | bytes 2359312 | tf_op jit(solution)/shard_map/all_gather | solution.py:125
  164.9 4.3 %copy.52 = bf16[1024,1152]{0,1:T(8,128)(2,1)} copy(bf16[1024,1152]{1,0:T(8,128)(2,1)} %all-gather.10.cloned.1.call-done) | data formatting | bytes 4718592 | tf_op jit(solution)/shard_map/all_gather | solution.py:125
  169.2 26.3 %all-gather.8.cloned.1.call-done = bf16[1024,1152]{1,0:T(8,128)(2,1)} async-done(((bf16[128,1152]{1,0:T(8,128)(2,1)}), bf16[1024,1152]{1,0:T(8,128)(2,1)}) %all-gather.8.cloned.1.call-update) | async-done | bytes 2359312 | tf_op jit(solution)/shard_map/all_gather | solution.py:126
  195.5 4.3 %copy.50 = bf16[1024,1152]{0,1:T(8,128)(2,1)} copy(bf16[1024,1152]{1,0:T(8,128)(2,1)} %all-gather.8.cloned.1.call-done) | data formatting | bytes 4718592 | tf_op jit(solution)/shard_map/all_gather | solution.py:126
  199.8 7.5 %fusion.84 = (f32[16,128]{1,0:T(8,128)S(1)}, bf16[16,128,1024]{2,1,0:T(8,128)(2,1)}) fusion(pred[128,1024]{1,0:T(8,128)(4,1)S(1)} %copy-done.2, bf16[128,16,72]{0,2,1:T(8,128)(2,1)S(1)} %bitcast.88, bf16[1024,16,72]{0,2,1:T(8,128)(2,1)} %bitcast.84), kind=kOutput, calls=%fused_computation.112 | convolution fusion | flops 314573824 | bytes 6987776 | tf_op jit(solution)/shard_map/sub | solution.py:39
  207.2 5.2 %fusion.26 = bf16[128,16,72]{0,2,1:T(8,128)(2,1)} fusion(bf16[1024,16,72]{0,2,1:T(8,128)(2,1)} %bitcast.85, bf16[16,128,1024]{2,1,0:T(8,128)(2,1)} %get-tuple-element.18, f32[128,16]{0,1:T(8,128)S(1)} %bitcast.95), kind=kOutput, calls=%fused_computation.31 | convolution fusion | flops 302284800 | bytes 6856704 | tf_op jit(solution)/shard_map/hqk,khd->qhd/dot_general | solution.py:42
  212.4 49.4 %all-gather.12.cloned.1.call-done = bf16[1152,1152]{0,1:T(8,128)(2,1)} async-done(((bf16[1152,72]{0,1:T(8,128)(2,1)}), bf16[1152,1152]{0,1:T(8,128)(2,1)}) %all-gather.12.cloned.1.call-update) | async-done | bytes 2654224 | tf_op jit(solution)/shard_map/all_gather | solution.py:117
  261.8 3.0 fusion.85
  265.0 2.2 fusion.41
  267.3 26.1 %all-gather.14.cloned.1.call-done = bf16[1024,1152]{1,0:T(8,128)(2,1)} async-done(((bf16[128,1152]{1,0:T(8,128)(2,1)}), bf16[1024,1152]{1,0:T(8,128)(2,1)}) %all-gather.14.cloned.1.call-update) | async-done | bytes 2359312 | tf_op jit(solution)/shard_map/all_gather | solution.py:140
  293.4 7.8 %convolution_convert_fusion = bf16[1024,1152]{1,0:T(8,128)(2,1)} fusion(bf16[576,1152]{1,0:T(8,128)(2,1)} %param.46, bf16[1024,1152]{1,0:T(8,128)(2,1)} %all-gather.14.cloned.1.call-done, bf16[1152,576]{0,1:T(8,128)(2,1)} %param.44, f32[576]{0:T(1024)S(1)} %convert_element_type.111), kind=kOutput, calls=%fused_computation.11 | convolution fusion | flops 2724986880 | bytes 7375104 | tf_op jit(solution)/shard_map/dot_general | solution.py:147
  301.9 36.9 %reduce-scatter.2.cloned.1.call-done = bf16[128,1152]{1,0:T(8,128)(2,1)} async-done(((bf16[1024,1152]{1,0:T(8,128)(2,1)}), bf16[128,1152]{1,0:T(8,128)(2,1)}) %reduce-scatter.2.cloned.1.call-update) | async-done | bytes 294928 | tf_op jit(solution)/shard_map/reduce_scatter | solution.py:146
  338.8 1.3 fusion.81
  340.4 2.2 convolution_add_fusion.6
  342.6 3.2 all-to-all-start.1
  345.9 3.7 %all-to-all-done.1 = f32[1,128,16]{1,0,2:T(1,128)S(1)} async-done(((f32[1,128,16]{1,0,2:T(1,128)}), f32[1,128,16]{1,0,2:T(1,128)S(1)}, u32[]{:S(2)}, u32[]{:S(2)}) %all-to-all-start.1) | async-done | bytes 8224 | tf_op jit(solution)/shard_map/all_to_all | solution.py:161
  (84 shorter events, 11.1 us)
Async XLA Ops:
  6.5 4.8 %copy-start = (bf16[1152,1152]{1,0:T(8,128)(2,1)S(1)}, bf16[1152,1152]{1,0:T(8,128)(2,1)}, u32[]{:S(2)}) copy-start(bf16[1152,1152]{1,0:T(8,128)(2,1)} %param.36) | copy-start | bytes 7962628
  6.5 111.0 %all-gather.6.cloned.1.call-start = ((), (), s32[]{:S(2)}) async-start(), calls=%async_computation.3 | async-start | bytes 8460288 | tf_op jit(solution)/shard_map/all_gather | solution.py:115
  13.2 15.4 %copy-start.10 = (s32[1,4]{1,0:T(1,128)S(1)}, s32[1,4]{1,0:T(1,128)}, u32[]{:S(2)}) copy-start(s32[1,4]{1,0:T(1,128)} %param.29) | copy-start | bytes 52
  13.2 15.5 %copy-start.14 = (u32[256]{0:T(256)S(1)}, u32[256]{0:T(256)}, u32[]{:S(2)}) copy-start(u32[256]{0:T(256)} %constant.70) | copy-start | bytes 3076
  13.2 17.4 %copy-start.11 = (bf16[216]{0:T(256)(128)(2,1)S(1)}, bf16[216]{0:T(256)(128)(2,1)}, u32[]{:S(2)}) copy-start(bf16[216]{0:T(256)(128)(2,1)} %param.41) | copy-start | bytes 1300
  13.2 17.7 %copy-start.12 = (bf16[72]{0:T(256)(128)(2,1)S(1)}, bf16[72]{0:T(256)(128)(2,1)}, u32[]{:S(2)}) copy-start(bf16[72]{0:T(256)(128)(2,1)} %param.43) | copy-start | bytes 436
  13.2 100.9 %copy-start.1 = (bf16[1,128,1152]{2,1,0:T(8,128)(2,1)S(1)}, bf16[1,128,1152]{2,1,0:T(8,128)(2,1)}, u32[]{:S(2)}) copy-start(bf16[1,128,1152]{2,1,0:T(8,128)(2,1)} %param.25) | copy-start | bytes 884740
  16.9 97.5 %all-to-all-start = ((bf16[16,4,576]{2,1,0:T(4,128)(2,1)}), bf16[16,4,576]{2,1,0:T(4,128)(2,1)S(1)}, u32[]{:S(2)}, u32[]{:S(2)}) async-start(bf16[16,4,576]{2,1,0:T(4,128)(2,1)} %reshape.143), calls=%async_computation | async-start | bytes 163840 | tf_op jit(solution)/shard_map/all_to_all | solution.py:102
  28.5 136.4 %all-gather.10.cloned.1.call-start = ((), (), s32[]{:S(2)}) async-start(), calls=%async_computation.5 | async-start | bytes 2654208 | tf_op jit(solution)/shard_map/all_gather | solution.py:125
  124.6 70.8 %all-gather.8.cloned.1.call-start = ((), (), s32[]{:S(2)}) async-start(), calls=%async_computation.4 | async-start | bytes 2654208 | tf_op jit(solution)/shard_map/all_gather | solution.py:126
  125.4 136.4 %all-gather.12.cloned.1.call-start = ((), (), s32[]{:S(2)}) async-start(), calls=%async_computation.6 | async-start | bytes 2820096 | tf_op jit(solution)/shard_map/all_gather | solution.py:117
  125.9 167.4 %all-gather.14.cloned.1.call-start = ((), (), s32[]{:S(2)}) async-start(), calls=%async_computation.7 | async-start | bytes 2654208 | tf_op jit(solution)/shard_map/all_gather | solution.py:140
  169.2 30.6 %copy-start.2 = (pred[128,1024]{1,0:T(8,128)(4,1)S(1)}, pred[128,1024]{1,0:T(8,128)(4,1)}, u32[]{:S(2)}) copy-start(pred[128,1024]{1,0:T(8,128)(4,1)} %broadcast_compare_fusion) | copy-start | bytes 393220
  264.8 2.5 copy-start.6
  267.2 71.7 %reduce-scatter.2.cloned.1.call-start = ((), (), s32[]{:S(2)}) async-start(), calls=%async_computation.8 | async-start | bytes 2654208 | tf_op jit(solution)/shard_map/reduce_scatter | solution.py:146
  301.2 0.7 copy-start.4
  301.2 0.7 copy-start.13
  301.2 39.2 %copy-start.3 = (bf16[1152,16]{0,1:T(8,128)(2,1)S(1)}, bf16[1152,16]{0,1:T(8,128)(2,1)}, u32[]{:S(2)}) copy-start(bf16[1152,16]{0,1:T(8,128)(2,1)} %param.48) | copy-start | bytes 110596
  301.9 43.9 %copy-start.7 = (f32[1,4]{1,0:T(1,128)S(1)}, f32[1,4]{1,0:T(1,128)}, u32[]{:S(2)}) copy-start(f32[1,4]{1,0:T(1,128)} %param.31) | copy-start | bytes 52
  301.9 44.0 %copy-start.8 = (f32[1,4]{1,0:T(1,128)S(1)}, f32[1,4]{1,0:T(1,128)}, u32[]{:S(2)}) copy-start(f32[1,4]{1,0:T(1,128)} %param.30) | copy-start | bytes 52
  301.9 44.0 %copy-start.9 = (f32[1,4]{1,0:T(1,128)S(1)}, f32[1,4]{1,0:T(1,128)}, u32[]{:S(2)}) copy-start(f32[1,4]{1,0:T(1,128)} %param.32) | copy-start | bytes 52
  301.9 47.7 %copy-start.5 = (f32[128,8]{0,1:T(8,128)S(1)}, f32[128,8]{0,1:T(8,128)}, u32[]{:S(2)}) copy-start(f32[128,8]{0,1:T(8,128)} %param.26) | copy-start | bytes 12292
  342.6 7.0 %all-to-all-start.1 = ((f32[1,128,16]{1,0,2:T(1,128)}), f32[1,128,16]{1,0,2:T(1,128)S(1)}, u32[]{:S(2)}, u32[]{:S(2)}) async-start(f32[1,128,16]{1,0,2:T(1,128)} %bitcast.16), calls=%async_computation.2 | async-start | bytes 16384 | tf_op jit(solution)/shard_map/all_to_all | solution.py:161
Sparse Core Ops, SparseCore 0:
  9.8 107.0 all-gather.5
  124.8 40.0 all-gather.9
  166.7 28.6 all-gather.7
  197.8 63.9 all-gather.11
  267.3 26.0 all-gather.13
  301.3 37.4 reduce-scatter.1
where the time goes:
time: 358 us; the launch traced here: 357 us
  waiting for transfers between devices  182 us (51%)
  blocking collectives  82.8 us (23%)
  matrix products  39.5 us (11%)
  starting transfers between devices  15.2 us (4%)
  between operations  15 us (4%)
  local copies, waits for them, and re-layouts  12.7 us (4%)
  other arithmetic  9.78 us (3%)
    unnamed x1, blocking collectives  82.8 us
    all_gather x1, waiting for transfers between devices, shards(): lax.all_gather(out_weight, 'req', axis=1, tiled=True)  49.4 us
    all_gather x1, waiting for transfers between devices, shards(): lax.all_gather(qkv[:, width:2 * width], 'mlp', axis=0, tiled=True)  37.7 us
    reduce_scatter x1, waiting for transfers between devices, shards(): lax.psum_scatter(jnp.dot(inner, down_weight, preferred_element_type=jnp.f...  36.9 us
    all_gather x1, waiting for transfers between devices, shards(): lax.all_gather(qkv[:, 2 * width:], 'mlp', axis=0, tiled=True)  26.3 us
    all_gather x1, waiting for transfers between devices, shards(): gathered = lax.all_gather(normed_mlp, 'mlp', axis=0, tiled=True)  26.1 us
    all_to_all x1, starting transfers between devices, shards(): lax.all_to_all(local_mod, 'req', split_axis=0, concat_axis=2, tiled=True)[0]  11.6 us
    dot_general x1, matrix products, shards(): jnp.dot(inner, down_weight, preferred_element_type=jnp.float32)  7.81 us
  transfers between devices with their start and end apart: 8, of which 6 were waited for; matrix products, arithmetic and copies ran while one was open for 10% of the time, Pallas kernels for 0%

commit v1 on v0

--- a/solution.py
+++ b/solution.py
@@ -114,7 +114,9 @@
     qkv_full, qkv_bias_full, out_full, out_bias_full = (
         lax.all_gather(qkv_weight, "req", axis=1, tiled=True),
         lax.all_gather(qkv_bias, "req", axis=0, tiled=True),
-        lax.all_gather(out_weight, "req", axis=1, tiled=True),
+        jnp.concatenate(
+            lax.all_to_all(jnp.stack([out_weight] * lax.axis_size("req")), "req", 0, 0), axis=1
+        ),
         lax.all_gather(out_bias, "req", axis=0, tiled=True),
     )
     qkv = (

time: 358 us -> 311 us (0.87)
  waiting for transfers between devices: 182 us -> 115 us
  starting transfers between devices: 15.2 us -> 33.7 us
    all_gather x1 -> x0, waiting for transfers between devices: 49.4 us -> none  [shards(): lax.all_gather(out_weight, 'req', axis=1, tiled=True)]
    all_gather x1, waiting for transfers between devices: 37.7 us -> 18 us  [shards(): lax.all_gather(qkv[:, width:2 * width], 'mlp', axis=0, tiled=True)]
    all_to_all x0 -> x1, starting transfers between devices: none -> 18.6 us  [shards(): lax.all_to_all(jnp.stack([out_weight] * lax.axis_size('req')), 'req', 0, 0)]
  transfers between devices with their start and end apart: 8 -> 8, of which waited for: 6 -> 5; matrix products, arithmetic and copies ran while one was open for 10% -> 12% of each run, Pallas kernels for 0% -> 0%
where the time goes in v1:
time: 311 us; the launch traced here: 310 us
  waiting for transfers between devices  115 us (37%)
  blocking collectives  82.8 us (27%)
  matrix products  39.5 us (13%)
  starting transfers between devices  33.7 us (11%)
  between operations  14.7 us (5%)
  local copies, waits for them, and re-layouts  14.4 us (5%)
  other arithmetic  9.78 us (3%)
    unnamed x1, blocking collectives  82.8 us
    reduce_scatter x1, waiting for transfers between devices, shards(): lax.psum_scatter(jnp.dot(inner, down_weight, preferred_element_type=jnp.f...  36.9 us
    all_gather x1, waiting for transfers between devices, shards(): gathered = lax.all_gather(normed_mlp, 'mlp', axis=0, tiled=True)  28.8 us
    all_gather x1, waiting for transfers between devices, shards(): lax.all_gather(qkv[:, 2 * width:], 'mlp', axis=0, tiled=True)  26.3 us
    all_to_all x1, starting transfers between devices, shards(): lax.all_to_all(jnp.stack([out_weight] * lax.axis_size('req')), 'req', 0, 0)  18.6 us
    all_gather x1, waiting for transfers between devices, shards(): lax.all_gather(qkv[:, width:2 * width], 'mlp', axis=0, tiled=True)  18 us
    all_to_all x1, starting transfers between devices, shards(): lax.all_to_all(local_mod, 'req', split_axis=0, concat_axis=2, tiled=True)[0]  11.6 us
    dot_general x1, matrix products, shards(): jnp.dot(inner, down_weight, preferred_element_type=jnp.float32)  7.81 us
  transfers between devices with their start and end apart: 8, of which 5 were waited for; matrix products, arithmetic and copies ran while one was open for 12% of the time, Pallas kernels for 0%

profile of v1, /device:TPU:8, one launch (start us, length us, event | category | flops | bytes accessed | tf_op | source)
XLA Modules:
  0.0 310.1 jit_solution(1463989959308202274)
XLA Ops:
  11.4 1.8 convolution_add_fusion.3
  13.2 3.0 fusion.29
  16.9 11.6 %all-to-all-start = ((bf16[16,4,576]{2,1,0:T(4,128)(2,1)}), bf16[16,4,576]{2,1,0:T(4,128)(2,1)S(1)}, u32[]{:S(2)}, u32[]{:S(2)}) async-start(bf16[16,4,576]{2,1,0:T(4,128)(2,1)} %reshape.151), calls=%async_computation | async-start | bytes 163840 | tf_op jit(solution)/shard_map/all_to_all | solution.py:102
  31.1 82.8 %all-reduce.2 = (bf16[3456]{0:T(1024)(128)(2,1)S(1)}, bf16[1152]{0:T(1024)(128)(2,1)S(1)}) all-reduce(bf16[3456]{0:T(1024)(128)(2,1)S(1)} %dynamic-update-slice, bf16[1152]{0:T(1024)(128)(2,1)S(1)} %dynamic-update-slice.1), channel_id=1, replica_groups=mesh['cfg'=2,'req'=16,'mlp'=8] {'req'}, use_global_device_ids=true, to_apply=%add | all-reduce | flops 4608 | bytes 18432
  114.6 3.0 fusion.67
  117.6 6.1 %fusion.2 = bf16[128,3456]{1,0:T(8,128)(2,1)S(1)} fusion(bf16[1152,3456]{0,1:T(8,128)(2,1)} %all-gather.5.cloned.1.call-done, f32[3456]{0:T(1024)S(1)} %convert_element_type.103, bf16[1,128,1152]{2,1,0:T(8,128)(2,1)S(1)} %copy-done.1, f32[128,9216]{1,0:T(8,128)} %fusion.67, f32[128]{0:T(128)S(1)} %add_rsqrt_fusion.2, f32[128]{0:T(128)S(1)} %broadcast_multiply_fusion.2), kind=kOutput, calls=%fused_computation.5 | convolution fusion | flops 1021132800 | bytes 10336768 | tf_op jit(solution)/shard_map/dot_general | solution.py:123
  123.7 0.9 fusion.83
  125.4 1.7 stack.2
  127.1 18.6 %all-to-all-start.1 = ((bf16[16,1152,72]{1,2,0:T(8,128)(2,1)}), bf16[16,1152,72]{1,2,0:T(8,128)(2,1)}, u32[]{:S(2)}, u32[]{:S(2)}) async-start(bf16[16,1152,72]{1,2,0:T(8,128)(2,1)} %stack.2), calls=%async_computation.1 | async-start | bytes 5308416 | tf_op jit(solution)/shard_map/all_to_all | solution.py:118
  146.9 18.0 %all-gather.9.cloned.1.call-done = bf16[1024,1152]{1,0:T(8,128)(2,1)} async-done(((bf16[128,1152]{1,0:T(8,128)(2,1)}), bf16[1024,1152]{1,0:T(8,128)(2,1)}) %all-gather.9.cloned.1.call-update) | async-done | bytes 2359312 | tf_op jit(solution)/shard_map/all_gather | solution.py:127
  164.9 4.3 %copy.53 = bf16[1024,1152]{0,1:T(8,128)(2,1)} copy(bf16[1024,1152]{1,0:T(8,128)(2,1)} %all-gather.9.cloned.1.call-done) | data formatting | bytes 4718592 | tf_op jit(solution)/shard_map/all_gather | solution.py:127
  169.2 26.3 %all-gather.7.cloned.1.call-done = bf16[1024,1152]{1,0:T(8,128)(2,1)} async-done(((bf16[128,1152]{1,0:T(8,128)(2,1)}), bf16[1024,1152]{1,0:T(8,128)(2,1)}) %all-gather.7.cloned.1.call-update) | async-done | bytes 2359312 | tf_op jit(solution)/shard_map/all_gather | solution.py:128
  195.5 4.3 %copy.51 = bf16[1024,1152]{0,1:T(8,128)(2,1)} copy(bf16[1024,1152]{1,0:T(8,128)(2,1)} %all-gather.7.cloned.1.call-done) | data formatting | bytes 4718592 | tf_op jit(solution)/shard_map/all_gather | solution.py:128
  199.8 7.5 %fusion.84 = (f32[16,128]{1,0:T(8,128)S(1)}, bf16[16,128,1024]{2,1,0:T(8,128)(2,1)}) fusion(pred[128,1024]{1,0:T(8,128)(4,1)S(1)} %copy-done.3, bf16[128,16,72]{0,2,1:T(8,128)(2,1)S(1)} %bitcast.91, bf16[1024,16,72]{0,2,1:T(8,128)(2,1)} %bitcast.87), kind=kOutput, calls=%fused_computation.112 | convolution fusion | flops 314573824 | bytes 6987776 | tf_op jit(solution)/shard_map/sub | solution.py:39
  207.2 5.2 %fusion.26 = bf16[128,16,72]{0,2,1:T(8,128)(2,1)} fusion(bf16[1024,16,72]{0,2,1:T(8,128)(2,1)} %bitcast.88, bf16[16,128,1024]{2,1,0:T(8,128)(2,1)} %get-tuple-element.18, f32[128,16]{0,1:T(8,128)S(1)} %bitcast.98), kind=kOutput, calls=%fused_computation.31 | convolution fusion | flops 302284800 | bytes 6856704 | tf_op jit(solution)/shard_map/hqk,khd->qhd/dot_general | solution.py:42
  212.4 3.0 fusion.85
  215.7 2.2 fusion.41
  217.9 28.8 %all-gather.11.cloned.1.call-done = bf16[1024,1152]{1,0:T(8,128)(2,1)} async-done(((bf16[128,1152]{1,0:T(8,128)(2,1)}), bf16[1024,1152]{1,0:T(8,128)(2,1)}) %all-gather.11.cloned.1.call-update) | async-done | bytes 2359312 | tf_op jit(solution)/shard_map/all_gather | solution.py:142
  246.7 7.8 %convolution_convert_fusion = bf16[1024,1152]{1,0:T(8,128)(2,1)} fusion(bf16[576,1152]{1,0:T(8,128)(2,1)} %param.46, bf16[1024,1152]{1,0:T(8,128)(2,1)} %all-gather.11.cloned.1.call-done, bf16[1152,576]{0,1:T(8,128)(2,1)} %param.44, f32[576]{0:T(1024)S(1)} %convert_element_type.111), kind=kOutput, calls=%fused_computation.11 | convolution fusion | flops 2724986880 | bytes 7375104 | tf_op jit(solution)/shard_map/dot_general | solution.py:149
  255.2 36.9 %reduce-scatter.2.cloned.1.call-done = bf16[128,1152]{1,0:T(8,128)(2,1)} async-done(((bf16[1024,1152]{1,0:T(8,128)(2,1)}), bf16[128,1152]{1,0:T(8,128)(2,1)}) %reduce-scatter.2.cloned.1.call-update) | async-done | bytes 294928 | tf_op jit(solution)/shard_map/reduce_scatter | solution.py:148
  292.2 1.3 fusion.81
  293.7 2.2 convolution_add_fusion.6
  295.9 3.2 %all-to-all-start.2 = ((f32[1,128,16]{1,0,2:T(1,128)}), f32[1,128,16]{1,0,2:T(1,128)S(1)}, u32[]{:S(2)}, u32[]{:S(2)}) async-start(f32[1,128,16]{1,0,2:T(1,128)} %bitcast.18), calls=%async_computation.3 | async-start | bytes 16384 | tf_op jit(solution)/shard_map/all_to_all | solution.py:163
  299.2 3.7 %all-to-all-done.2 = f32[1,128,16]{1,0,2:T(1,128)S(1)} async-done(((f32[1,128,16]{1,0,2:T(1,128)}), f32[1,128,16]{1,0,2:T(1,128)S(1)}, u32[]{:S(2)}, u32[]{:S(2)}) %all-to-all-start.2) | async-done | bytes 8224 | tf_op jit(solution)/shard_map/all_to_all | solution.py:163
  (86 shorter events, 11.3 us)
Async XLA Ops:
  6.5 4.8 %copy-start = (bf16[1152,1152]{1,0:T(8,128)(2,1)S(1)}, bf16[1152,1152]{1,0:T(8,128)(2,1)}, u32[]{:S(2)}) copy-start(bf16[1152,1152]{1,0:T(8,128)(2,1)} %param.36) | copy-start | bytes 7962628
  6.5 111.0 %all-gather.5.cloned.1.call-start = ((), (), s32[]{:S(2)}) async-start(), calls=%async_computation.4 | async-start | bytes 8460288 | tf_op jit(solution)/shard_map/all_gather | solution.py:115
  13.2 15.4 %copy-start.11 = (s32[1,4]{1,0:T(1,128)S(1)}, s32[1,4]{1,0:T(1,128)}, u32[]{:S(2)}) copy-start(s32[1,4]{1,0:T(1,128)} %param.29) | copy-start | bytes 52
  13.2 15.5 %copy-start.15 = (u32[256]{0:T(256)S(1)}, u32[256]{0:T(256)}, u32[]{:S(2)}) copy-start(u32[256]{0:T(256)} %constant.70) | copy-start | bytes 3076
  13.2 17.4 %copy-start.12 = (bf16[216]{0:T(256)(128)(2,1)S(1)}, bf16[216]{0:T(256)(128)(2,1)}, u32[]{:S(2)}) copy-start(bf16[216]{0:T(256)(128)(2,1)} %param.41) | copy-start | bytes 1300
  13.2 17.7 %copy-start.13 = (bf16[72]{0:T(256)(128)(2,1)S(1)}, bf16[72]{0:T(256)(128)(2,1)}, u32[]{:S(2)}) copy-start(bf16[72]{0:T(256)(128)(2,1)} %param.43) | copy-start | bytes 436
  13.2 100.9 %copy-start.1 = (bf16[1,128,1152]{2,1,0:T(8,128)(2,1)S(1)}, bf16[1,128,1152]{2,1,0:T(8,128)(2,1)}, u32[]{:S(2)}) copy-start(bf16[1,128,1152]{2,1,0:T(8,128)(2,1)} %param.25) | copy-start | bytes 884740
  16.9 97.5 %all-to-all-start = ((bf16[16,4,576]{2,1,0:T(4,128)(2,1)}), bf16[16,4,576]{2,1,0:T(4,128)(2,1)S(1)}, u32[]{:S(2)}, u32[]{:S(2)}) async-start(bf16[16,4,576]{2,1,0:T(4,128)(2,1)} %reshape.151), calls=%async_computation | async-start | bytes 163840 | tf_op jit(solution)/shard_map/all_to_all | solution.py:102
  28.5 136.4 %all-gather.9.cloned.1.call-start = ((), (), s32[]{:S(2)}) async-start(), calls=%async_computation.6 | async-start | bytes 2654208 | tf_op jit(solution)/shard_map/all_gather | solution.py:127
  123.7 1.7 copy-start.2
  124.6 70.8 %all-gather.7.cloned.1.call-start = ((), (), s32[]{:S(2)}) async-start(), calls=%async_computation.5 | async-start | bytes 2654208 | tf_op jit(solution)/shard_map/all_gather | solution.py:128
  127.1 85.3 %all-to-all-start.1 = ((bf16[16,1152,72]{1,2,0:T(8,128)(2,1)}), bf16[16,1152,72]{1,2,0:T(8,128)(2,1)}, u32[]{:S(2)}, u32[]{:S(2)}) async-start(bf16[16,1152,72]{1,2,0:T(8,128)(2,1)} %stack.2), calls=%async_computation.1 | async-start | bytes 5308416 | tf_op jit(solution)/shard_map/all_to_all | solution.py:118
  145.7 101.0 %all-gather.11.cloned.1.call-start = ((), (), s32[]{:S(2)}) async-start(), calls=%async_computation.7 | async-start | bytes 2654208 | tf_op jit(solution)/shard_map/all_gather | solution.py:142
  169.2 30.6 %copy-start.3 = (pred[128,1024]{1,0:T(8,128)(4,1)S(1)}, pred[128,1024]{1,0:T(8,128)(4,1)}, u32[]{:S(2)}) copy-start(pred[128,1024]{1,0:T(8,128)(4,1)} %broadcast_compare_fusion) | copy-start | bytes 393220
  215.4 2.5 copy-start.7
  217.8 74.3 %reduce-scatter.2.cloned.1.call-start = ((), (), s32[]{:S(2)}) async-start(), calls=%async_computation.8 | async-start | bytes 2654208 | tf_op jit(solution)/shard_map/reduce_scatter | solution.py:148
  254.5 0.7 copy-start.5
  254.5 0.7 copy-start.14
  254.5 39.2 %copy-start.4 = (bf16[1152,16]{0,1:T(8,128)(2,1)S(1)}, bf16[1152,16]{0,1:T(8,128)(2,1)}, u32[]{:S(2)}) copy-start(bf16[1152,16]{0,1:T(8,128)(2,1)} %param.48) | copy-start | bytes 110596
  255.2 43.9 %copy-start.8 = (f32[1,4]{1,0:T(1,128)S(1)}, f32[1,4]{1,0:T(1,128)}, u32[]{:S(2)}) copy-start(f32[1,4]{1,0:T(1,128)} %param.31) | copy-start | bytes 52
  255.2 44.0 %copy-start.9 = (f32[1,4]{1,0:T(1,128)S(1)}, f32[1,4]{1,0:T(1,128)}, u32[]{:S(2)}) copy-start(f32[1,4]{1,0:T(1,128)} %param.30) | copy-start | bytes 52
  255.2 44.0 %copy-start.10 = (f32[1,4]{1,0:T(1,128)S(1)}, f32[1,4]{1,0:T(1,128)}, u32[]{:S(2)}) copy-start(f32[1,4]{1,0:T(1,128)} %param.32) | copy-start | bytes 52
  255.2 47.7 %copy-start.6 = (f32[128,8]{0,1:T(8,128)S(1)}, f32[128,8]{0,1:T(8,128)}, u32[]{:S(2)}) copy-start(f32[128,8]{0,1:T(8,128)} %param.26) | copy-start | bytes 12292
  295.9 7.0 %all-to-all-start.2 = ((f32[1,128,16]{1,0,2:T(1,128)}), f32[1,128,16]{1,0,2:T(1,128)S(1)}, u32[]{:S(2)}, u32[]{:S(2)}) async-start(f32[1,128,16]{1,0,2:T(1,128)} %bitcast.18), calls=%async_computation.3 | async-start | bytes 16384 | tf_op jit(solution)/shard_map/all_to_all | solution.py:163
Sparse Core Ops, SparseCore 0:
  9.8 107.0 all-gather.4
  124.8 40.0 all-gather.8
  166.7 28.6 all-gather.6
  218.0 28.6 all-gather.10
  254.6 37.4 reduce-scatter.1
